TPU v7x, 128 devices: a whole 4x4x4 slice. The times are simulated.
128 devices in a mesh: sec: 4 (over z_hi, core), pts: 32 (over x, z_lo, y).
Axes of the slice: x: 4, y: 4, z: 4 (z_hi: 2, z_lo: 2; z = z_hi * 2 + z_lo), core: 2. Of those that a mesh axis runs over, the one named last changes fastest.
Arguments:
- points: bfloat16 [4, 32768, 1024], P('sec', 'pts'), may hold values from -10 to 10
- counts: int32 [4, 32], P('sec', 'pts'), may hold values from 256 to 1024, as said below
- input_gain: float32 [4, 1024], P('sec'), may hold values from 0.1 to 1.9
- key_weight: bfloat16 [4, 1024, 1024], P('sec', 'pts'), may hold values from -0.375 to 0.375
- value_weight: bfloat16 [4, 1024, 1024], P('sec', 'pts'), may hold values from -0.375 to 0.375
- query_weight: bfloat16 [1024, 1024], replicated, may hold values from -0.1875 to 0.1875
- output_weight: bfloat16 [1024, 1024], replicated, may hold values from -0.75 to 0.75
- middle_gain: float32 [1024], replicated, may hold values from 0.1 to 1.9
- up_weight: bfloat16 [1024, 4096], P(None, 'sec'), may hold values from -0.1875 to 0.1875
- down_weight: bfloat16 [4096, 1024], P('sec'), may hold values from -0.09375 to 0.09375
Outputs:
- updated: bfloat16 [32768, 1024], P('pts', 'sec')
Inputs may be any that keep to these rules, and one draw needn't show every extreme that they name: `counts`: each block has 1024 slots; in every section some block is full.
All inputs are finite; a program needn't handle non-finite values.
Results may differ from a plain program's by a relative error of at most 0.0049.
Values may be sent and summed in bfloat16 or wider, within the bound.
No kernel may reach another device: no remote copies, remote signals or barrier semaphores. Data moves between devices by JAX's collectives and lax.ppermute only.
A program may use at most 128 MiB of HBM per device.

v0:
```python
import jax
import jax.numpy as jnp
from jax import lax
from jax.sharding import PartitionSpec as P

HEAD_DIM = 128


def broadcast(value, axis, root):
    mine = lax.axis_index(axis) == root
    return lax.psum(jnp.where(mine, value, jnp.zeros_like(value)), axis)


def layer_normalizer(values, gain):
    mean = jnp.mean(values, axis=-1, keepdims=True)
    centred = values - mean
    spread = jnp.mean(centred * centred, axis=-1, keepdims=True)
    return centred * lax.rsqrt(spread + 1e-05) * gain


def feature_map(values):
    return jax.nn.elu(values) + 1.0


def on_device(
    points,
    counts,
    input_gain,
    key_weight,
    value_weight,
    query_weight,
    output_weight,
    middle_gain,
    up_weight,
    down_weight,
):
    block = points[0]
    rows = block.shape[0]
    width = block.shape[1]
    heads = width // HEAD_DIM
    sections = lax.axis_size("sec")
    normed = layer_normalizer(block.astype(jnp.float32), input_gain[0]).astype(jnp.bfloat16)

    def add_rows(piece):
        return jnp.dot(normed, piece[0], preferred_element_type=jnp.float32)

    summed_keys = add_rows(lax.all_gather(key_weight, "pts", axis=1, tiled=True))
    value_sums = add_rows(lax.all_gather(value_weight, "pts", axis=1, tiled=True))
    valid = jnp.arange(rows) < counts[0, 0]
    key_feats = feature_map(summed_keys).astype(jnp.bfloat16)
    key_feats = jnp.where(valid[:, None], key_feats, jnp.zeros_like(key_feats))
    value_rows = value_sums.astype(jnp.bfloat16)
    local_state = jnp.einsum(
        "yzl,yzn->zln",
        key_feats.reshape(rows, heads, HEAD_DIM),
        value_rows.reshape(rows, heads, HEAD_DIM),
        preferred_element_type=jnp.float32,
    ).reshape(width, HEAD_DIM)
    local_total = jnp.sum(key_feats.astype(jnp.float32), axis=0)
    part_state, part_total = (
        lax.all_gather(local_state[None], "sec", axis=0, tiled=True),
        lax.all_gather(local_total[None], "sec", axis=0, tiled=True),
    )
    state_matrices, totals = lax.psum((part_state, part_total), "pts")
    query_feats = feature_map(
        jnp.dot(normed, query_weight, preferred_element_type=jnp.float32)
    ).astype(jnp.bfloat16)
    query_feats = lax.optimization_barrier(query_feats)
    per_head_queries = query_feats.astype(jnp.float32).reshape(rows, heads, HEAD_DIM)
    state_heads = state_matrices.reshape(sections, heads, HEAD_DIM, HEAD_DIM)
    total_heads = totals.reshape(sections, heads, HEAD_DIM)
    numerator = jnp.einsum(
        "rhk,shkv->srhv", per_head_queries, state_heads, precision=lax.Precision.HIGHEST
    )
    denom = jnp.einsum(
        "rhk,shk->srh", per_head_queries, total_heads, precision=lax.Precision.HIGHEST
    )
    attended = (
        jnp.sum(numerator / denom[:, :, :, None], axis=0).reshape(rows, width).astype(jnp.bfloat16)
    )
    mixed = block.astype(jnp.float32) + jnp.dot(
        attended, output_weight, preferred_element_type=jnp.float32
    )
    centred = layer_normalizer(mixed, middle_gain).astype(jnp.bfloat16)
    shared = broadcast(centred, "sec", sections - 1)
    hidden = jax.nn.gelu(
        jnp.dot(shared, up_weight, preferred_element_type=jnp.float32), approximate=True
    ).astype(jnp.bfloat16)
    is_query = (lax.axis_index("sec") == sections - 1).astype(jnp.float32)
    term = jnp.dot(hidden, down_weight, preferred_element_type=jnp.float32) + is_query * mixed
    return lax.psum_scatter(term, "sec", scatter_dimension=1, tiled=True).astype(jnp.bfloat16)


def solution(mesh):
    placed = (
        P("sec", "pts", None),
        P("sec", "pts"),
        P("sec", None),
        P("sec", "pts", None),
        P("sec", "pts", None),
        P(),
        P(),
        P(),
        P(None, "sec"),
        P("sec", None),
    )
    return jax.shard_map(
        on_device, mesh=mesh, in_specs=placed, out_specs=P("pts", "sec"), check_vma=False
    )
```

profile of v0, /device:TPU:1, one launch (start us, length us, event | category | flops | bytes accessed | tf_op | source)
XLA Modules:
  0.0 817.7 jit_solution(15731884587893129483)
XLA Ops:
  6.5 0.7 all-gather.7.cloned.1.call-update
  8.7 4.0 copy.41
  12.7 2.1 convert_reduce_fusion
  15.5 127.3 %all-gather.7.cloned.1.call-done = bf16[1,1024,1024]{2,1,0:T(8,128)(2,1)} async-done(((bf16[1,32,1024]{2,1,0:T(8,128)(2,1)}), bf16[1,1024,1024]{2,1,0:T(8,128)(2,1)}) %all-gather.7.cloned.1.call-update) | async-done | bytes 2097168 | tf_op jit(solution)/shard_map/all_gather | solution.py:48
  142.8 6.2 fusion.45
  149.1 148.2 %all-gather.5.cloned.1.call-done = bf16[1,1024,1024]{2,1,0:T(8,128)(2,1)} async-done(((bf16[1,32,1024]{2,1,0:T(8,128)(2,1)}), bf16[1,1024,1024]{2,1,0:T(8,128)(2,1)}) %all-gather.5.cloned.1.call-update) | async-done | bytes 2097168 | tf_op jit(solution)/shard_map/all_gather | solution.py:47
  297.2 6.8 convert_reduce_fusion.1
  304.0 1.5 fusion.61
  305.6 49.3 %all-gather.9.cloned.1.call-done = f32[4,1024,128]{2,1,0:T(8,128)} async-done(((f32[1,1024,128]{2,1,0:T(8,128)}), f32[4,1024,128]{2,1,0:T(8,128)}) %all-gather.9.cloned.1.call-update) | async-done | bytes 2097168 | tf_op jit(solution)/shard_map/all_gather | solution.py:61
  354.9 2.9 copy.43
  358.1 7.6 fusion.24
  365.6 6.8 all-gather
  372.4 131.4 %psum.22 = f32[4,8,128]{2,0,1:T(4,128)S(1)} all-reduce(f32[4,8,128]{2,0,1:T(4,128)S(1)} %copy.48), channel_id=1, replica_groups=mesh['sec'=4,'pts'=32] {'pts'}, use_global_device_ids=true, to_apply=%region_4.5 | all-reduce | flops 4096 | bytes 32768 | tf_op jit(solution)/shard_map/psum | solution.py:64
  503.8 2.5 convolution_bitcast_fusion
  506.4 142.2 %all-reduce.3.cloned.1.call-done = f32[4,8,128,128]{2,3,0,1:T(8,128)} async-done(((f32[4,8,128,128]{2,3,0,1:T(8,128)}), f32[4,8,128,128]{2,3,0,1:T(8,128)}) %all-reduce.3.cloned.1.call-update) | async-done | bytes 2097168 | tf_op jit(solution)/shard_map/psum | solution.py:64
  648.5 9.9 %fusion = bf16[1024,8,128]{0,2,1:T(8,128)(2,1)S(1)} fusion(f32[4,8,128,128]{2,3,0,1:T(8,128)} %all-reduce.3.cloned.1.call-done, bf16[1024,8,128,1]{0,2,3,1:T(8,128)(2,1)} %bitcast.71, f32[4,1024,8]{1,0,2:T(4,128)S(1)} %convolution_bitcast_fusion), kind=kOutput, calls=%fused_computation.1 | convolution fusion | flops 6449790976 | bytes 6422528 | tf_op jit(solution)/shard_map/rhk,shkv->srhv/dot_general | solution.py:72
  658.5 2.6 fusion.58
  661.6 1.4 copy-done.3
  663.1 2.0 fusion.25
  665.3 81.6 %all-reduce.5.cloned.1.call-done = bf16[1024,1024]{0,1:T(8,128)(2,1)} async-done(((bf16[1024,1024]{0,1:T(8,128)(2,1)}), bf16[1024,1024]{0,1:T(8,128)(2,1)}) %all-reduce.5.cloned.1.call-update) | async-done | bytes 2097168 | tf_op jit(solution)/shard_map/psum | solution.py:11
  746.9 11.3 %multiply_add_fusion = f32[1024,1024]{0,1:T(8,128)} fusion(f32[1024,1024]{0,1:T(8,128)} %copy-done.3, f32[]{:T(128)S(6)} %convert_element_type.62, bf16[1024,1024]{1,0:T(8,128)(2,1)} %param.19, bf16[1024,1024]{0,1:T(8,128)(2,1)} %all-reduce.5.cloned.1.call-done, bf16[1024,1024]{1,0:T(8,128)(2,1)} %param.18), kind=kOutput, calls=%fused_computation.34 | convolution fusion | flops 4306501632 | bytes 14680068 | tf_op jit(solution)/shard_map/dot_general | solution.py:90
  758.2 50.3 %reduce-scatter.2.cloned.1.call-done = f32[1024,256]{0,1:T(8,128)} async-done(((f32[1024,1024]{0,1:T(8,128)}), f32[1024,256]{0,1:T(8,128)}) %reduce-scatter.2.cloned.1.call-update) | async-done | bytes 1048592 | tf_op jit(solution)/shard_map/reduce_scatter | solution.py:91
  808.5 1.3 convert_element_type.63
  809.8 1.0 copy.56
  (32 shorter events, 2.6 us)
Async XLA Ops:
  6.5 651.9 %copy-start = (bf16[1024,1024]{1,0:T(8,128)(2,1)S(1)}, bf16[1024,1024]{1,0:T(8,128)(2,1)}, u32[]{:S(2)}) copy-start(bf16[1024,1024]{1,0:T(8,128)(2,1)} %param.16) | copy-start | bytes 6291460
  6.5 136.3 %all-gather.7.cloned.1.call-start = ((), (), s32[]{:S(2)}) async-start(), calls=%async_computation.2 | async-start | bytes 2162688 | tf_op jit(solution)/shard_map/all_gather | solution.py:48
  7.3 290.0 %all-gather.5.cloned.1.call-start = ((), (), s32[]{:S(2)}) async-start(), calls=%async_computation.1 | async-start | bytes 2162688 | tf_op jit(solution)/shard_map/all_gather | solution.py:47
  8.0 346.9 %all-gather.9.cloned.1.call-start = ((), (), s32[]{:S(2)}) async-start(), calls=%async_computation.3 | async-start | bytes 2621440 | tf_op jit(solution)/shard_map/all_gather | solution.py:61
  12.7 2.2 copy-start.1
  12.7 130.2 %copy-start.6 = (f32[1,1024]{1,0:T(1,128)S(1)}, f32[1,1024]{1,0:T(1,128)}, u32[]{:S(2)}) copy-start(f32[1,1024]{1,0:T(1,128)} %param.12) | copy-start | bytes 12292
  297.2 6.8 copy-start.4
  305.5 343.0 %all-reduce.3.cloned.1.call-start = ((), (), s32[]{:S(2)}) async-start(), calls=%async_computation.4 | async-start | bytes 4194304 | tf_op jit(solution)/shard_map/psum | solution.py:64
  357.8 389.1 %all-reduce.5.cloned.1.call-start = ((), (), s32[]{:S(2)}) async-start(), calls=%async_computation.5 | async-start | bytes 4194304 | tf_op jit(solution)/shard_map/psum | solution.py:11
  648.5 10.0 %copy-start.2 = (bf16[1,1024,1024]{1,2,0:T(8,128)(2,1)S(1)}, bf16[1,1024,1024]{1,2,0:T(8,128)(2,1)}, u32[]{:S(2)}) copy-start(bf16[1,1024,1024]{1,2,0:T(8,128)(2,1)} %copy.41) | copy-start | bytes 6291460
  661.1 1.9 copy-start.3
  661.1 1.9 copy-start.5
  665.1 143.5 %reduce-scatter.2.cloned.1.call-start = ((), (), s32[]{:S(2)}) async-start(), calls=%async_computation.6 | async-start | bytes 5242880 | tf_op jit(solution)/shard_map/reduce_scatter | solution.py:91
Sparse Core Ops, SparseCore 0:
  9.0 133.8 all-gather.6
  144.5 152.6 all-gather.4
  305.7 49.2 all-gather.8
  357.9 290.5 all-reduce.2
  665.2 81.6 all-reduce.4
  758.3 50.1 reduce-scatter.1
where the time goes:
time: 818 us
  waiting for transfers between devices  600 us (73%)
  blocking collectives  138 us (17%)
  matrix products  48.4 us (6%)
  between operations  14.2 us (2%)
  local copies, waits for them, and re-layouts  9.38 us (1%)
    all_gather x1, waiting for transfers between devices, on_device(): lax.all_gather(key_weight, 'pts', axis=1, tiled=True)  148 us
    psum x1, waiting for transfers between devices, on_device(): state_matrices, totals = lax.psum((part_state, part_total), 'pts')  142 us
    psum x1, blocking collectives, on_device(): state_matrices, totals = lax.psum((part_state, part_total), 'pts')  131 us
    all_gather x1, waiting for transfers between devices, on_device(): lax.all_gather(value_weight, 'pts', axis=1, tiled=True)  127 us
    psum x1, waiting for transfers between devices, broadcast(): return lax.psum(jnp.where(mine, value, jnp.zeros_like(value)), axis)  81.6 us
    reduce_scatter x1, waiting for transfers between devices, on_device(): lax.psum_scatter(term, 'sec', scatter_dimension=1, tiled=True)  50.3 us
    all_gather x1, waiting for transfers between devices, on_device(): lax.all_gather(local_state[None], 'sec', axis=0, tiled=True)  49.3 us
  transfers between devices with their start and end apart: 6, of which 6 were waited for; matrix products, arithmetic and copies ran while one was open for 3% of the time, Pallas kernels for 0%

commit v1 on v0

--- a/solution.py
+++ b/solution.py
@@ -8,7 +8,7 @@
 
 def broadcast(value, axis, root):
     mine = lax.axis_index(axis) == root
-    return lax.psum(jnp.where(mine, value, jnp.zeros_like(value)), axis)
+    return jnp.sum(jax.lax.all_gather(jnp.where(mine, value, jnp.zeros_like(value)), axis), 0)
 
 
 def layer_normalizer(values, gain):

time: 818 us -> 850 us (1.039)
  local copies, waits for them, and re-layouts: 9.38 us -> 23.9 us
  other arithmetic: 6.49 us -> 19.4 us
    all_gather x0 -> x1, waiting for transfers between devices: none -> 85.2 us  [broadcast(): jax.lax.all_gather(jnp.where(mine, value, jnp.zeros_like(value)), axis)]
    psum x1 -> x0, waiting for transfers between devices: 81.6 us -> none  [broadcast(): return lax.psum(jnp.where(mine, value, jnp.zeros_like(value)), axis)]
    all_gather x0 -> x1, local copies, waits for them, and re-layouts: none -> 14.6 us  [broadcast(): jax.lax.all_gather(jnp.where(mine, value, jnp.zeros_like(value)), axis)]
    reduce_sum x0 -> x1, other arithmetic: none -> 12.9 us  [broadcast(): jnp.sum(jax.lax.all_gather(jnp.where(mine, value, jnp.zeros_like(value)),...]
where the time goes in v1:
time: 850 us; the launch traced here: 849 us
  waiting for transfers between devices  604 us (71%)
  blocking collectives  138 us (16%)
  matrix products  48.4 us (6%)
  local copies, waits for them, and re-layouts  23.9 us (3%)
  other arithmetic  19.4 us (2%)
  between operations  14.2 us (2%)
    all_gather x1, waiting for transfers between devices, on_device(): lax.all_gather(key_weight, 'pts', axis=1, tiled=True)  148 us
    psum x1, waiting for transfers between devices, on_device(): state_matrices, totals = lax.psum((part_state, part_total), 'pts')  142 us
    psum x1, blocking collectives, on_device(): state_matrices, totals = lax.psum((part_state, part_total), 'pts')  131 us
    all_gather x1, waiting for transfers between devices, on_device(): lax.all_gather(value_weight, 'pts', axis=1, tiled=True)  127 us
    all_gather x1, waiting for transfers between devices, broadcast(): jax.lax.all_gather(jnp.where(mine, value, jnp.zeros_like(value)), axis)  85.2 us
    reduce_scatter x1, waiting for transfers between devices, on_device(): lax.psum_scatter(term, 'sec', scatter_dimension=1, tiled=True)  50.4 us
    all_gather x1, waiting for transfers between devices, on_device(): lax.all_gather(local_state[None], 'sec', axis=0, tiled=True)  49.3 us
  transfers between devices with their start and end apart: 6, of which 6 were waited for; matrix products, arithmetic and copies ran while one was open for 3% of the time, Pallas kernels for 0%

profile of v1, /device:TPU:1, one launch (start us, length us, event | category | flops | bytes accessed | tf_op | source)
XLA Modules:
  0.0 848.8 jit_solution(16009192727181119187)
XLA Ops:
  8.7 4.0 copy.41
  12.7 2.1 convert_reduce_fusion
  15.5 127.3 %all-gather.9.cloned.1.call-done = bf16[1,1024,1024]{2,1,0:T(8,128)(2,1)} async-done(((bf16[1,32,1024]{2,1,0:T(8,128)(2,1)}), bf16[1,1024,1024]{2,1,0:T(8,128)(2,1)}) %all-gather.9.cloned.1.call-update) | async-done | bytes 2097168 | tf_op jit(solution)/shard_map/all_gather | solution.py:48
  142.8 6.2 fusion.45
  149.1 148.2 %all-gather.7.cloned.1.call-done = bf16[1,1024,1024]{2,1,0:T(8,128)(2,1)} async-done(((bf16[1,32,1024]{2,1,0:T(8,128)(2,1)}), bf16[1,1024,1024]{2,1,0:T(8,128)(2,1)}) %all-gather.7.cloned.1.call-update) | async-done | bytes 2097168 | tf_op jit(solution)/shard_map/all_gather | solution.py:47
  297.2 6.8 convert_reduce_fusion.1
  304.0 1.5 fusion.61
  305.6 49.3 %all-gather.11.cloned.1.call-done = f32[4,1024,128]{2,1,0:T(8,128)} async-done(((f32[1,1024,128]{2,1,0:T(8,128)}), f32[4,1024,128]{2,1,0:T(8,128)}) %all-gather.11.cloned.1.call-update) | async-done | bytes 2097168 | tf_op jit(solution)/shard_map/all_gather | solution.py:61
  354.9 2.9 copy.43
  358.1 7.6 fusion.24
  365.6 6.8 all-gather
  372.4 131.4 %psum.15 = f32[4,8,128]{2,0,1:T(4,128)S(1)} all-reduce(f32[4,8,128]{2,0,1:T(4,128)S(1)} %copy.48), channel_id=1, replica_groups=mesh['sec'=4,'pts'=32] {'pts'}, use_global_device_ids=true, to_apply=%region_4.5 | all-reduce | flops 4096 | bytes 32768 | tf_op jit(solution)/shard_map/psum | solution.py:64
  503.8 2.5 convolution_bitcast_fusion
  506.4 142.2 %all-reduce.2.cloned.1.call-done = f32[4,8,128,128]{2,3,0,1:T(8,128)} async-done(((f32[4,8,128,128]{2,3,0,1:T(8,128)}), f32[4,8,128,128]{2,3,0,1:T(8,128)}) %all-reduce.2.cloned.1.call-update) | async-done | bytes 2097168 | tf_op jit(solution)/shard_map/psum | solution.py:64
  648.5 9.9 %fusion = bf16[1024,8,128]{0,2,1:T(8,128)(2,1)S(1)} fusion(f32[4,8,128,128]{2,3,0,1:T(8,128)} %all-reduce.2.cloned.1.call-done, bf16[1024,8,128,1]{0,2,3,1:T(8,128)(2,1)} %bitcast.73, f32[4,1024,8]{1,0,2:T(4,128)S(1)} %convolution_bitcast_fusion), kind=kOutput, calls=%fused_computation.1 | convolution fusion | flops 6449790976 | bytes 6422528 | tf_op jit(solution)/shard_map/rhk,shkv->srhv/dot_general | solution.py:72
  658.5 2.6 fusion.58
  661.6 1.4 copy-done.3
  663.0 2.0 fusion.25
  665.4 85.2 %all-gather.13.cloned.1.call-done = bf16[4096,1024]{0,1:T(8,128)(2,1)} async-done(((bf16[1024,1024]{0,1:T(8,128)(2,1)}), bf16[4096,1024]{0,1:T(8,128)(2,1)}) %all-gather.13.cloned.1.call-update) | async-done | bytes 8388624 | tf_op jit(solution)/shard_map/all_gather | solution.py:11
  750.6 14.6 %reshape.96 = bf16[4,1024,1024]{1,0,2:T(4,128)(2,1)} reshape(bf16[4096,1024]{0,1:T(8,128)(2,1)} %all-gather.13.cloned.1.call-done) | data formatting | bytes 16777216 | tf_op jit(solution)/shard_map/all_gather | solution.py:11
  765.1 12.9 %reduce_sum.72 = bf16[1024,1024]{0,1:T(8,128)(2,1)} reduce(bf16[4,1024,1024]{1,0,2:T(4,128)(2,1)} %reshape.96, bf16[]{:T(256)} %constant.31.clone.1), dimensions={0}, to_apply=%region_8.9 | reduce | flops 3145728 | bytes 10485762 | tf_op jit(solution)/shard_map/reduce_sum | solution.py:11
  778.0 11.3 %multiply_add_fusion = f32[1024,1024]{0,1:T(8,128)} fusion(f32[1024,1024]{0,1:T(8,128)} %copy-done.3, f32[]{:T(128)S(6)} %convert_element_type.64, bf16[1024,1024]{1,0:T(8,128)(2,1)} %param.19, bf16[1024,1024]{0,1:T(8,128)(2,1)} %reduce_sum.72, bf16[1024,1024]{1,0:T(8,128)(2,1)} %param.18), kind=kOutput, calls=%fused_computation.34 | convolution fusion | flops 4306501632 | bytes 14680068 | tf_op jit(solution)/shard_map/dot_general | solution.py:90
  789.3 50.4 %reduce-scatter.2.cloned.1.call-done = f32[1024,256]{0,1:T(8,128)} async-done(((f32[1024,1024]{0,1:T(8,128)}), f32[1024,256]{0,1:T(8,128)}) %reduce-scatter.2.cloned.1.call-update) | async-done | bytes 1048592 | tf_op jit(solution)/shard_map/reduce_scatter | solution.py:91
  839.7 1.3 convert_element_type.65
  (34 shorter events, 4.3 us)
Async XLA Ops:
  6.5 651.9 %copy-start = (bf16[1024,1024]{1,0:T(8,128)(2,1)S(1)}, bf16[1024,1024]{1,0:T(8,128)(2,1)}, u32[]{:S(2)}) copy-start(bf16[1024,1024]{1,0:T(8,128)(2,1)} %param.16) | copy-start | bytes 6291460
  6.5 136.3 %all-gather.9.cloned.1.call-start = ((), (), s32[]{:S(2)}) async-start(), calls=%async_computation.2 | async-start | bytes 2162688 | tf_op jit(solution)/shard_map/all_gather | solution.py:48
  7.3 290.0 %all-gather.7.cloned.1.call-start = ((), (), s32[]{:S(2)}) async-start(), calls=%async_computation.1 | async-start | bytes 2162688 | tf_op jit(solution)/shard_map/all_gather | solution.py:47
  8.0 346.9 %all-gather.11.cloned.1.call-start = ((), (), s32[]{:S(2)}) async-start(), calls=%async_computation.3 | async-start | bytes 2621440 | tf_op jit(solution)/shard_map/all_gather | solution.py:61
  12.7 2.2 copy-start.1
  12.7 130.2 %copy-start.6 = (f32[1,1024]{1,0:T(1,128)S(1)}, f32[1,1024]{1,0:T(1,128)}, u32[]{:S(2)}) copy-start(f32[1,1024]{1,0:T(1,128)} %param.12) | copy-start | bytes 12292
  297.2 6.8 copy-start.4
  305.5 343.0 %all-reduce.2.cloned.1.call-start = ((), (), s32[]{:S(2)}) async-start(), calls=%async_computation.4 | async-start | bytes 4194304 | tf_op jit(solution)/shard_map/psum | solution.py:64
  357.8 392.8 %all-gather.13.cloned.1.call-start = ((), (), s32[]{:S(2)}) async-start(), calls=%async_computation.6 | async-start | bytes 10485760 | tf_op jit(solution)/shard_map/all_gather | solution.py:11
  648.5 10.0 %copy-start.2 = (bf16[1,1024,1024]{1,2,0:T(8,128)(2,1)S(1)}, bf16[1,1024,1024]{1,2,0:T(8,128)(2,1)}, u32[]{:S(2)}) copy-start(bf16[1,1024,1024]{1,2,0:T(8,128)(2,1)} %copy.41) | copy-start | bytes 6291460
  661.1 1.9 copy-start.3
  661.1 1.9 copy-start.5
  665.1 174.6 %reduce-scatter.2.cloned.1.call-start = ((), (), s32[]{:S(2)}) async-start(), calls=%async_computation.5 | async-start | bytes 5242880 | tf_op jit(solution)/shard_map/reduce_scatter | solution.py:91
Sparse Core Ops, SparseCore 0:
  9.0 133.8 all-gather.8
  144.5 152.6 all-gather.6
  305.7 49.2 all-gather.10
  357.9 290.5 all-reduce.1
  665.2 85.2 all-gather.12
  789.4 50.2 reduce-scatter.1
